TPU v7x, 512 devices: a whole 4x4x16 slice. The times are simulated.
512 devices in a mesh: seq: 64 (over y, z_lo, core), tp: 8 (over z_hi, x).
Axes of the slice: x: 4, y: 4, z: 16 (z_hi: 2, z_lo: 8; z = z_hi * 8 + z_lo), core: 2. Of those that a mesh axis runs over, the one named last changes fastest.
Arguments:
- tokens: bfloat16 [16384, 4096], P('seq', 'tp'), may hold values from -6 to 6
- ln_gain: float32 [4096], replicated, may hold values from 0.1 to 1.9
- ln_bias: float32 [4096], replicated, may hold values from -3 to 3
- w_qkv: bfloat16 [4096, 16, 3, 128], P('seq', 'tp'), may hold values from -3 to 3
- w_out: bfloat16 [16, 128, 4096], P('tp', None, 'seq'), may hold values from -0.25 to 0.25
- layer_scale: float32 [4096], P('tp'), may hold values from 0.5 to 2
- grids: int32 [14], replicated, may hold values from 24 to 40, as said below
- offsets: int32 [15], replicated, may hold values from 0 to 15302, as said below
Outputs:
- merged: bfloat16 [16384, 4, 4096], P('seq', None, 'tp')
Inputs may be any that keep to these rules, and one draw needn't show every extreme that they name: `grids`: every side is even and some image has side exactly 40. Of images 2k and 2k + 1, one side is drawn and the other is the largest even side of at most 40 whose square keeps the two squares' sum within 2176. offsets[0] = 0 and offsets[s + 1] = offsets[s] + 5 + grids[s] * grids[s].
All inputs are finite; a program needn't handle non-finite values.
Results may differ from a plain program's by a relative error of at most 0.015.
Values may be sent and summed in bfloat16 or wider, within the bound.
No kernel may reach another device: no remote copies, remote signals or barrier semaphores. Data moves between devices by JAX's collectives and lax.ppermute only.
A program may use at most 64 MiB of HBM per device.

v0:
```python
import math
import jax
import jax.numpy as jnp
from jax import lax
from jax.sharding import PartitionSpec as P

HALO = 48
REACH = 7


def from_behind(shard, axis, by):
    count = lax.axis_size(axis)
    pairs = [(i, i + by) for i in range(count) if 0 <= i + by < count]
    return lax.ppermute(shard, axis, pairs)


def layout_rows(row_ids, offsets, grids, row_count):
    images = grids.shape[0]
    image_ends = offsets[1:]
    segment = jnp.sum((row_ids[:, None] >= image_ends[None, :]).astype(jnp.int32), axis=1)
    inside = (row_ids >= 0) & (row_ids < row_count) & (segment < images)
    onehot = (
        jnp.minimum(segment, images - 1)[:, None] == jnp.arange(images, dtype=jnp.int32)[None, :]
    ).astype(jnp.int32)
    image_start = jnp.sum(onehot * offsets[None, :-1], axis=1)
    grid_side = jnp.sum(onehot * grids[None, :], axis=1)
    position = row_ids - image_start
    is_patch = inside & (position >= 5)
    patch_index = jnp.maximum(position - 5, 0)
    return (segment, inside, is_patch, patch_index // grid_side, patch_index % grid_side, grid_side)


def rotate(vectors, is_patch, grid_row, grid_col, grid_side):
    quarter = vectors.shape[-1] // 4
    frequency = 2.0 * math.pi * jnp.power(100.0, -jnp.arange(quarter, dtype=jnp.float32) / quarter)
    side_float = grid_side.astype(jnp.float32)
    coord_row = (2 * grid_row + 1).astype(jnp.float32) / side_float - 1.0
    coord_col = (2 * grid_col + 1).astype(jnp.float32) / side_float - 1.0
    angles_row = jnp.where(is_patch[:, None], coord_row[:, None] * frequency[None, :], 0.0)
    angles_col = jnp.where(is_patch[:, None], coord_col[:, None] * frequency[None, :], 0.0)

    def rotate_half(block_vals, angles):
        first_half = block_vals[..., :quarter]
        second_half = block_vals[..., quarter:]
        cosine = jnp.cos(angles)[:, None, :]
        sine_part = jnp.sin(angles)[:, None, :]
        return jnp.concatenate(
            [
                first_half * cosine - second_half * sine_part,
                second_half * cosine + first_half * sine_part,
            ],
            axis=-1,
        )

    return jnp.concatenate(
        [
            rotate_half(vectors[..., : 2 * quarter], angles_row),
            rotate_half(vectors[..., 2 * quarter :], angles_col),
        ],
        axis=-1,
    )


def attend_blocks(query_matrix, kv_blocks, key_segment, key_inside, query_segment, query_inside):
    logit_scale_factor = 1.0 / math.sqrt(query_matrix.shape[-1])
    rows_here = query_matrix.shape[0]
    heads_here = query_matrix.shape[1]

    def block_scores(block_of_keys, segment_block, inside_block):
        attention_logits = (
            jnp.einsum(
                "ecn,dcn->ced", query_matrix, block_of_keys, preferred_element_type=jnp.float32
            )
            * logit_scale_factor
        )
        allowed = (
            query_inside[:, None]
            & inside_block[None, :]
            & (query_segment[:, None] == segment_block[None, :])
        )
        return (jnp.where(allowed[None], attention_logits, -1e30), allowed)

    def max_step(carry, input_block_rows):
        row_max, row_total = carry
        masked, allowed = block_scores(
            input_block_rows[0][:, 0], input_block_rows[1], input_block_rows[2]
        )
        new_max = jnp.maximum(row_max, jnp.max(masked, axis=2, keepdims=True))
        exp_terms = jnp.where(allowed[None], jnp.exp(masked - new_max), 0.0)
        row_total = row_total * jnp.exp(row_max - new_max) + jnp.sum(
            exp_terms, axis=2, keepdims=True
        )
        return ((new_max, row_total), None)

    start_max = jnp.full((heads_here, rows_here, 1), -1e30, jnp.float32)
    start_total = jnp.zeros((heads_here, rows_here, 1), jnp.float32)
    (row_max, row_total), _ = lax.scan(
        max_step, (start_max, start_total), (kv_blocks, key_segment, key_inside)
    )
    row_total = jnp.where(query_inside[None, :, None], row_total, 1.0)

    def sum_step(running, input_block_rows):
        masked, allowed = block_scores(
            input_block_rows[0][:, 0], input_block_rows[1], input_block_rows[2]
        )
        exp_terms = jnp.where(allowed[None], jnp.exp(masked - row_max), 0.0)
        softmax_probabilities = (exp_terms / row_total).astype(jnp.bfloat16)
        return (
            running
            + jnp.einsum(
                "vgm,mvb->gvb",
                softmax_probabilities,
                input_block_rows[0][:, 1],
                preferred_element_type=jnp.float32,
            ),
            None,
        )

    start_sum = jnp.zeros((rows_here, heads_here, query_matrix.shape[2]), jnp.float32)
    attended_output, _ = lax.scan(sum_step, start_sum, (kv_blocks, key_segment, key_inside))
    attended_output = jnp.where(query_inside[:, None, None], attended_output, 0.0)
    return attended_output.astype(jnp.bfloat16)


def body(tokens, ln_gain, ln_bias, w_qkv, w_out, layer_scale, grids, offsets):
    rows_here = tokens.shape[0]
    row_count = rows_here * lax.axis_size("seq")
    first_row = lax.axis_index("seq") * rows_here
    gathered = lax.all_gather(tokens, "tp", axis=1, tiled=True)
    widened = gathered.astype(jnp.float32)
    average = jnp.mean(widened, axis=-1, keepdims=True)
    spread_sq = jnp.mean(jnp.square(widened - average), axis=-1, keepdims=True)
    normed = ((widened - average) * lax.rsqrt(spread_sq + 1e-06) * ln_gain + ln_bias).astype(
        jnp.bfloat16
    )
    qkv_sums = jnp.einsum(
        "td,dhcf->thcf",
        normed,
        lax.all_gather(w_qkv, "seq", axis=0, tiled=True),
        preferred_element_type=jnp.float32,
    )
    row_ids = first_row + jnp.arange(rows_here, dtype=jnp.int32)
    segment, inside, is_patch, grid_row, grid_col, grid_side = layout_rows(
        row_ids, offsets, grids, row_count
    )
    query_matrix = rotate(qkv_sums[:, :, 0], is_patch, grid_row, grid_col, grid_side).astype(
        jnp.bfloat16
    )
    roped_keys = rotate(qkv_sums[:, :, 1], is_patch, grid_row, grid_col, grid_side).astype(
        jnp.bfloat16
    )
    values = qkv_sums[:, :, 2].astype(jnp.bfloat16)
    key_value = jnp.stack([roped_keys, values], axis=1)
    block_count = 2 * REACH + 1
    pieces = []
    for block_slot in range(block_count):
        distance = REACH - block_slot
        if distance == 0:
            pieces.append(key_value)
        else:
            pieces.append(from_behind(key_value, "seq", distance))
    kv_blocks = jnp.stack(pieces, axis=0)
    key_rows = first_row - REACH * rows_here + jnp.arange(block_count * rows_here, dtype=jnp.int32)
    key_layout = layout_rows(key_rows, offsets, grids, row_count)
    key_segment = key_layout[0].reshape(block_count, rows_here)
    key_inside = key_layout[1].reshape(block_count, rows_here)
    attended_output = attend_blocks(
        query_matrix, kv_blocks, key_segment, key_inside, segment, inside
    )
    projected = jnp.einsum(
        "thf,hfc->tc",
        attended_output,
        lax.all_gather(w_out, "seq", axis=2, tiled=True),
        preferred_element_type=jnp.float32,
    )
    head_share = lax.psum_scatter(
        projected.astype(jnp.bfloat16), "tp", scatter_dimension=1, tiled=True
    ).astype(jnp.float32)
    layer_out = (tokens.astype(jnp.float32) + layer_scale * head_share).astype(jnp.bfloat16)
    next_rows = from_behind(layer_out[:HALO], "seq", -1)
    extended = jnp.concatenate([layer_out, next_rows], axis=0)
    is_corner = is_patch & (grid_row % 2 == 0) & (grid_col % 2 == 0)
    local_ids = jnp.arange(rows_here, dtype=jnp.int32)
    corner_index = jnp.stack(
        [local_ids, local_ids + 1, local_ids + grid_side, local_ids + grid_side + 1], axis=1
    )
    corner_index = jnp.clip(corner_index, 0, extended.shape[0] - 1)
    merged = jnp.take(extended, corner_index, axis=0)
    return jnp.where(is_corner[:, None, None], merged, jnp.zeros_like(merged))


def solution(mesh):
    placed = (
        P("seq", "tp"),
        P(),
        P(),
        P("seq", "tp", None, None),
        P("tp", None, "seq"),
        P("tp"),
        P(),
        P(),
    )
    return jax.shard_map(
        body, mesh=mesh, in_specs=placed, out_specs=P("seq", None, "tp"), check_vma=False
    )
```

profile of v0, /device:TPU:1, one launch (start us, length us, event | category | flops | bytes accessed | tf_op | source)
XLA Modules:
  0.0 669.1 jit_solution(13033573889273032923)
XLA Ops:
  7.3 1.5 copy.39
  12.0 115.7 %all-gather.4.cloned.1.call-done = bf16[256,4096]{1,0:T(8,128)(2,1)} async-done(((bf16[256,512]{1,0:T(8,128)(2,1)}), bf16[256,4096]{1,0:T(8,128)(2,1)}) %all-gather.4.cloned.1.call-update) | async-done | bytes 2097168 | tf_op jit(solution)/shard_map/all_gather | solution.py:129
  127.7 2.1 convert_reduce_fusion
  129.9 2.3 fusion.24
  132.1 122.1 %all-gather.6.cloned.1.call-done = bf16[4096,2,3,128]{3,0,2,1:T(8,128)(2,1)} async-done(((bf16[64,2,3,128]{3,0,2,1:T(8,128)(2,1)}), bf16[4096,2,3,128]{3,0,2,1:T(8,128)(2,1)}) %all-gather.6.cloned.1.call-update) | async-done | bytes 6291472 | tf_op jit(solution)/shard_map/all_gather | solution.py:139
  254.3 5.7 fusion.29
  260.2 6.1 collective-permute-start
  266.3 2.4 collective-permute-start.1
  268.7 3.8 collective-permute-start.2
  272.5 4.0 collective-permute-start.3
  276.4 3.2 collective-permute-start.4
  279.9 20.5 %collective-permute-start.5 = (bf16[256,2,2,128]{0,3,2,1:T(8,128)(2,1)S(1)}, bf16[256,2,2,128]{0,3,2,1:T(8,128)(2,1)S(1)}, u32[]{:S(2)}, u32[]{:S(2)}) collective-permute-start(bf16[256,2,2,128]{0,3,2,1:T(8,128)(2,1)S(1)} %pad_maximum_fusion.1), channel_id=1, source_target_pairs={{0,16},{8,24},{16,32},{24,40},{32,48},{40,56},{48,64},{56,72},{64,... | collective-permute-start | bytes 786440 | tf_op jit(solution)/shard_map/ppermute | solution.py:14
  301.1 5.2 collective-permute-start.6
  307.1 1.9 collective-permute-start.7
  309.7 1.3 collective-permute-start.8
  311.7 1.3 collective-permute-start.9
  313.7 1.3 collective-permute-start.10
  315.8 1.3 collective-permute-start.11
  318.5 22.9 %collective-permute-done.7 = bf16[256,2,2,128]{0,3,2,1:T(8,128)(2,1)S(1)} collective-permute-done((bf16[256,2,2,128]{0,3,2,1:T(8,128)(2,1)S(1)}, bf16[256,2,2,128]{0,3,2,1:T(8,128)(2,1)S(1)}, u32[]{:S(2)}, u32[]{:S(2)}) %collective-permute-start.7) | collective-permute-done | bytes 262176 | tf_op jit(solution)/shard_map/ppermute | solution.py:14
  341.4 1.3 collective-permute-start.12
  343.4 3.6 collective-permute-done.8
  347.0 1.3 collective-permute-start.13
  349.0 21.4 %collective-permute-done.9 = bf16[256,2,2,128]{0,3,2,1:T(8,128)(2,1)S(1)} collective-permute-done((bf16[256,2,2,128]{0,3,2,1:T(8,128)(2,1)S(1)}, bf16[256,2,2,128]{0,3,2,1:T(8,128)(2,1)S(1)}, u32[]{:S(2)}, u32[]{:S(2)}) %collective-permute-start.9) | collective-permute-done | bytes 262176 | tf_op jit(solution)/shard_map/ppermute | solution.py:14
  371.8 27.3 %collective-permute-done.11 = bf16[256,2,2,128]{0,3,2,1:T(8,128)(2,1)S(1)} collective-permute-done((bf16[256,2,2,128]{0,3,2,1:T(8,128)(2,1)S(1)}, bf16[256,2,2,128]{0,3,2,1:T(8,128)(2,1)S(1)}, u32[]{:S(2)}, u32[]{:S(2)}) %collective-permute-start.11) | collective-permute-done | bytes 262176 | tf_op jit(solution)/shard_map/ppermute | solution.py:14
  399.8 11.2 %collective-permute-done.12 = bf16[256,2,2,128]{0,3,2,1:T(8,128)(2,1)S(1)} collective-permute-done((bf16[256,2,2,128]{0,3,2,1:T(8,128)(2,1)S(1)}, bf16[256,2,2,128]{0,3,2,1:T(8,128)(2,1)S(1)}, u32[]{:S(2)}, u32[]{:S(2)}) %collective-permute-start.12) | collective-permute-done | bytes 262176 | tf_op jit(solution)/shard_map/ppermute | solution.py:14
  411.8 28.7 %collective-permute-done.13 = bf16[256,2,2,128]{0,3,2,1:T(8,128)(2,1)S(1)} collective-permute-done((bf16[256,2,2,128]{0,3,2,1:T(8,128)(2,1)S(1)}, bf16[256,2,2,128]{0,3,2,1:T(8,128)(2,1)S(1)}, u32[]{:S(2)}, u32[]{:S(2)}) %collective-permute-start.13) | collective-permute-done | bytes 262176 | tf_op jit(solution)/shard_map/ppermute | solution.py:14
  441.2 6.3 copy.44
  447.5 24.1 %while.24 = (s32[]{:T(128)}, f32[2,256,1]{1,0,2:T(2,128)S(1)}, f32[2,256,1]{1,0,2:T(2,128)S(1)}, pred[256]{0:T(512)(128)(4,1)S(1)}, pred[15,256]{1,0:T(8,128)(4,...) while((s32[]{:T(128)}, f32[2,256,1]{1,0,2:T(2,128)S(1)}, ...), condition=%wide.region_9.10_spmd.clone, body=%wide.region_6.9_spmd.clone.sunk | while | flops 34540032 | bytes 2063492 | solution.py:97
  447.7 1.0 dynamic-slice_bitcast_fusion.4
  450.9 1.0 dynamic-slice_bitcast_fusion.4
  452.5 1.0 dynamic-slice_bitcast_fusion.4
  454.1 1.0 dynamic-slice_bitcast_fusion.4
  455.7 1.0 dynamic-slice_bitcast_fusion.4
  457.3 1.0 dynamic-slice_bitcast_fusion.4
  458.9 1.0 dynamic-slice_bitcast_fusion.4
  460.5 1.0 dynamic-slice_bitcast_fusion.4
  463.7 1.0 dynamic-slice_bitcast_fusion.4
  465.4 1.0 dynamic-slice_bitcast_fusion.4
  471.6 25.9 %while.25 = (s32[]{:T(128)}, f32[256,2,128]{0,2,1:T(8,128)S(1)}, bf16[15,256,2,2,128]{4,1,3,2,0:T(8,128)(2,1)}, pred[256]{0:T(512)(128)(4,1)S(1)}, pred[15,256]{...) while((s32[]{:T(128)}, f32[256,2,128]{0,2,1:T(8,128)S(1)}, ...), condition=%wide.region_11.12_spmd.clone, body=%wide.region_10.11_spmd.clone.sunk | while | flops 68222976 | bytes 1582219 | solution.py:120
  471.8 1.0 dynamic-slice_bitcast_fusion.5
  497.5 5.0 all-gather.8.cloned.1.call-done
  502.5 3.7 fusion.21
  506.6 142.4 %reduce-scatter.2.cloned.1.call-done = bf16[256,512]{1,0:T(8,128)(2,1)} async-done(((bf16[256,4096]{1,0:T(8,128)(2,1)}), bf16[256,512]{1,0:T(8,128)(2,1)}) %reduce-scatter.2.cloned.1.call-update) | async-done | bytes 262160 | tf_op jit(solution)/shard_map/reduce_scatter | solution.py:176
  649.0 1.0 add_convert_fusion
  650.1 4.2 collective-permute-start.14
  654.5 1.0 collective-permute-done.14
  655.5 4.0 gather_fusion
  659.8 2.8 select_select_fusion
  (281 shorter events, 53.6 us)
Async XLA Ops:
  6.5 247.8 %copy-start.4 = (f32[4096]{0:T(1024)S(1)}, f32[4096]{0:T(1024)}, u32[]{:S(2)}) copy-start(f32[4096]{0:T(1024)} %param.13) | copy-start | bytes 49156
  6.5 247.8 %copy-start.3 = (f32[4096]{0:T(1024)S(1)}, f32[4096]{0:T(1024)}, u32[]{:S(2)}) copy-start(f32[4096]{0:T(1024)} %param.14) | copy-start | bytes 49156
  6.5 121.2 %all-gather.4.cloned.1.call-start = ((), (), s32[]{:S(2)}) async-start(), calls=%async_computation.1 | async-start | bytes 2359296 | tf_op jit(solution)/shard_map/all_gather | solution.py:129
  7.3 247.0 %all-gather.6.cloned.1.call-start = ((), (), s32[]{:S(2)}) async-start(), calls=%async_computation.2 | async-start | bytes 6389760 | tf_op jit(solution)/shard_map/all_gather | solution.py:139
  8.9 493.6 %all-gather.8.cloned.1.call-start = ((), (), s32[]{:S(2)}) async-start(), calls=%async_computation.3 | async-start | bytes 2129920 | tf_op jit(solution)/shard_map/all_gather | solution.py:173
  9.6 639.4 %reduce-scatter.2.cloned.1.call-start = ((), (), s32[]{:S(2)}) async-start(), calls=%async_computation.4 | async-start | bytes 2359296 | tf_op jit(solution)/shard_map/reduce_scatter | solution.py:176
  127.7 126.5 %copy-start = (bf16[256,4096]{1,0:T(8,128)(2,1)S(1)}, bf16[256,4096]{1,0:T(8,128)(2,1)}, u32[]{:S(2)}) copy-start(bf16[256,4096]{1,0:T(8,128)(2,1)} %all-gather.4.cloned.1.call-done) | copy-start | bytes 6291460
  260.2 19.7 %collective-permute-start = (bf16[256,2,2,128]{0,3,2,1:T(8,128)(2,1)S(1)}, bf16[256,2,2,128]{0,3,2,1:T(8,128)(2,1)S(1)}, u32[]{:S(2)}, u32[]{:S(2)}) collective-permute-start(bf16[256,2,2,128]{0,3,2,1:T(8,128)(2,1)S(1)} %pad_maximum_fusion.1), channel_id=1, source_target_pairs={{0,56},{8,64},{16,72},{24,80},{32,88},{40,96},{48,104},{56,112},{6... | collective-permute-start | bytes 786440 | tf_op jit(solution)/shard_map/ppermute | solution.py:14
  266.3 34.8 %collective-permute-start.1 = (bf16[256,2,2,128]{0,3,2,1:T(8,128)(2,1)S(1)}, bf16[256,2,2,128]{0,3,2,1:T(8,128)(2,1)S(1)}, u32[]{:S(2)}, u32[]{:S(2)}) collective-permute-start(bf16[256,2,2,128]{0,3,2,1:T(8,128)(2,1)S(1)} %pad_maximum_fusion.1), channel_id=1, source_target_pairs={{0,48},{8,56},{16,64},{24,72},{32,80},{40,88},{48,96},{56,104},{64... | collective-permute-start | bytes 786440 | tf_op jit(solution)/shard_map/ppermute | solution.py:14
  268.7 38.4 %collective-permute-start.2 = (bf16[256,2,2,128]{0,3,2,1:T(8,128)(2,1)S(1)}, bf16[256,2,2,128]{0,3,2,1:T(8,128)(2,1)S(1)}, u32[]{:S(2)}, u32[]{:S(2)}) collective-permute-start(bf16[256,2,2,128]{0,3,2,1:T(8,128)(2,1)S(1)} %pad_maximum_fusion.1), channel_id=1, source_target_pairs={{0,40},{8,48},{16,56},{24,64},{32,72},{40,80},{48,88},{56,96},{64,... | collective-permute-start | bytes 786440 | tf_op jit(solution)/shard_map/ppermute | solution.py:14
  272.5 37.2 %collective-permute-start.3 = (bf16[256,2,2,128]{0,3,2,1:T(8,128)(2,1)S(1)}, bf16[256,2,2,128]{0,3,2,1:T(8,128)(2,1)S(1)}, u32[]{:S(2)}, u32[]{:S(2)}) collective-permute-start(bf16[256,2,2,128]{0,3,2,1:T(8,128)(2,1)S(1)} %pad_maximum_fusion.1), channel_id=1, source_target_pairs={{0,32},{8,40},{16,48},{24,56},{32,64},{40,72},{48,80},{56,88},{64,... | collective-permute-start | bytes 786440 | tf_op jit(solution)/shard_map/ppermute | solution.py:14
  276.4 35.3 %collective-permute-start.4 = (bf16[256,2,2,128]{0,3,2,1:T(8,128)(2,1)S(1)}, bf16[256,2,2,128]{0,3,2,1:T(8,128)(2,1)S(1)}, u32[]{:S(2)}, u32[]{:S(2)}) collective-permute-start(bf16[256,2,2,128]{0,3,2,1:T(8,128)(2,1)S(1)} %pad_maximum_fusion.1), channel_id=1, source_target_pairs={{0,24},{8,32},{16,40},{24,48},{32,56},{40,64},{48,72},{56,80},{64,... | collective-permute-start | bytes 786440 | tf_op jit(solution)/shard_map/ppermute | solution.py:14
  279.9 33.9 %collective-permute-start.5 = (bf16[256,2,2,128]{0,3,2,1:T(8,128)(2,1)S(1)}, bf16[256,2,2,128]{0,3,2,1:T(8,128)(2,1)S(1)}, u32[]{:S(2)}, u32[]{:S(2)}) collective-permute-start(bf16[256,2,2,128]{0,3,2,1:T(8,128)(2,1)S(1)} %pad_maximum_fusion.1), channel_id=1, source_target_pairs={{0,16},{8,24},{16,32},{24,40},{32,48},{40,56},{48,64},{56,72},{64,... | collective-permute-start | bytes 786440 | tf_op jit(solution)/shard_map/ppermute | solution.py:14
  301.1 14.7 %collective-permute-start.6 = (bf16[256,2,2,128]{0,3,2,1:T(8,128)(2,1)S(1)}, bf16[256,2,2,128]{0,3,2,1:T(8,128)(2,1)S(1)}, u32[]{:S(2)}, u32[]{:S(2)}) collective-permute-start(bf16[256,2,2,128]{0,3,2,1:T(8,128)(2,1)S(1)} %pad_maximum_fusion.1), channel_id=1, source_target_pairs={{0,8},{8,16},{16,24},{24,32},{32,40},{40,48},{48,56},{56,64},{64,7... | collective-permute-start | bytes 786440 | tf_op jit(solution)/shard_map/ppermute | solution.py:14
  307.1 34.3 %collective-permute-start.7 = (bf16[256,2,2,128]{0,3,2,1:T(8,128)(2,1)S(1)}, bf16[256,2,2,128]{0,3,2,1:T(8,128)(2,1)S(1)}, u32[]{:S(2)}, u32[]{:S(2)}) collective-permute-start(bf16[256,2,2,128]{0,3,2,1:T(8,128)(2,1)S(1)} %pad_maximum_fusion.1), channel_id=1, source_target_pairs={{8,0},{16,8},{24,16},{32,24},{40,32},{48,40},{56,48},{64,56},{72,6... | collective-permute-start | bytes 786440 | tf_op jit(solution)/shard_map/ppermute | solution.py:14
  309.7 37.3 %collective-permute-start.8 = (bf16[256,2,2,128]{0,3,2,1:T(8,128)(2,1)S(1)}, bf16[256,2,2,128]{0,3,2,1:T(8,128)(2,1)S(1)}, u32[]{:S(2)}, u32[]{:S(2)}) collective-permute-start(bf16[256,2,2,128]{0,3,2,1:T(8,128)(2,1)S(1)} %pad_maximum_fusion.1), channel_id=1, source_target_pairs={{16,0},{24,8},{32,16},{40,24},{48,32},{56,40},{64,48},{72,56},{80,... | collective-permute-start | bytes 786440 | tf_op jit(solution)/shard_map/ppermute | solution.py:14
  311.7 58.6 %collective-permute-start.9 = (bf16[256,2,2,128]{0,3,2,1:T(8,128)(2,1)S(1)}, bf16[256,2,2,128]{0,3,2,1:T(8,128)(2,1)S(1)}, u32[]{:S(2)}, u32[]{:S(2)}) collective-permute-start(bf16[256,2,2,128]{0,3,2,1:T(8,128)(2,1)S(1)} %pad_maximum_fusion.1), channel_id=1, source_target_pairs={{24,0},{32,8},{40,16},{48,24},{56,32},{64,40},{72,48},{80,56},{88,... | collective-permute-start | bytes 786440 | tf_op jit(solution)/shard_map/ppermute | solution.py:14
  313.7 57.4 %collective-permute-start.10 = (bf16[256,2,2,128]{0,3,2,1:T(8,128)(2,1)S(1)}, bf16[256,2,2,128]{0,3,2,1:T(8,128)(2,1)S(1)}, u32[]{:S(2)}, u32[]{:S(2)}) collective-permute-start(bf16[256,2,2,128]{0,3,2,1:T(8,128)(2,1)S(1)} %pad_maximum_fusion.1), channel_id=1, source_target_pairs={{32,0},{40,8},{48,16},{56,24},{64,32},{72,40},{80,48},{88,56},{96,... | collective-permute-start | bytes 786440 | tf_op jit(solution)/shard_map/ppermute | solution.py:14
  315.8 83.4 %collective-permute-start.11 = (bf16[256,2,2,128]{0,3,2,1:T(8,128)(2,1)S(1)}, bf16[256,2,2,128]{0,3,2,1:T(8,128)(2,1)S(1)}, u32[]{:S(2)}, u32[]{:S(2)}) collective-permute-start(bf16[256,2,2,128]{0,3,2,1:T(8,128)(2,1)S(1)} %pad_maximum_fusion.1), channel_id=1, source_target_pairs={{40,0},{48,8},{56,16},{64,24},{72,32},{80,40},{88,48},{96,56},{104... | collective-permute-start | bytes 786440 | tf_op jit(solution)/shard_map/ppermute | solution.py:14
  341.4 69.7 %collective-permute-start.12 = (bf16[256,2,2,128]{0,3,2,1:T(8,128)(2,1)S(1)}, bf16[256,2,2,128]{0,3,2,1:T(8,128)(2,1)S(1)}, u32[]{:S(2)}, u32[]{:S(2)}) collective-permute-start(bf16[256,2,2,128]{0,3,2,1:T(8,128)(2,1)S(1)} %pad_maximum_fusion.1), channel_id=1, source_target_pairs={{48,0},{56,8},{64,16},{72,24},{80,32},{88,40},{96,48},{104,56},{11... | collective-permute-start | bytes 786440 | tf_op jit(solution)/shard_map/ppermute | solution.py:14
  347.0 93.5 %collective-permute-start.13 = (bf16[256,2,2,128]{0,3,2,1:T(8,128)(2,1)S(1)}, bf16[256,2,2,128]{0,3,2,1:T(8,128)(2,1)S(1)}, u32[]{:S(2)}, u32[]{:S(2)}) collective-permute-start(bf16[256,2,2,128]{0,3,2,1:T(8,128)(2,1)S(1)} %pad_maximum_fusion.1), channel_id=1, source_target_pairs={{56,0},{64,8},{72,16},{80,24},{88,32},{96,40},{104,48},{112,56},{1... | collective-permute-start | bytes 786440 | tf_op jit(solution)/shard_map/ppermute | solution.py:14
  497.5 151.5 %copy-start.1 = (bf16[256,512]{1,0:T(8,128)(2,1)S(1)}, bf16[256,512]{1,0:T(8,128)(2,1)}, u32[]{:S(2)}) copy-start(bf16[256,512]{1,0:T(8,128)(2,1)} %param.12) | copy-start | bytes 786436
  497.5 151.5 %copy-start.2 = (f32[512]{0:T(512)S(1)}, f32[512]{0:T(512)}, u32[]{:S(2)}) copy-start(f32[512]{0:T(512)} %param.17) | copy-start | bytes 6148
  650.1 5.4 collective-permute-start.14
Sparse Core Ops, SparseCore 0:
  10.4 117.3 all-gather.3
  129.9 124.3 all-gather.5
  256.5 246.0 all-gather.7
  507.0 141.9 reduce-scatter.1
where the time goes:
time: 671 us; the launch traced here: 669 us
  waiting for transfers between devices  503 us (75%)
  starting transfers between devices  59.1 us (9%)
  local copies, waits for them, and re-layouts  54.2 us (8%)
  matrix products  21 us (3%)
  other arithmetic  17 us (3%)
  between operations  13.6 us (2%)
    reduce_scatter x1, waiting for transfers between devices, body(): lax.psum_scatter(projected.astype(jnp.bfloat16), 'tp', scatter_dimension=...  142 us
    all_gather x1, waiting for transfers between devices, body(): lax.all_gather(w_qkv, 'seq', axis=0, tiled=True)  122 us
    ppermute x15, waiting for transfers between devices, from_behind(): return lax.ppermute(shard, axis, pairs)  116 us
    all_gather x1, waiting for transfers between devices, body(): gathered = lax.all_gather(tokens, 'tp', axis=1, tiled=True)  116 us
    ppermute x15, starting transfers between devices, from_behind(): return lax.ppermute(shard, axis, pairs)  58.9 us
    squeeze x30, local copies, waits for them, and re-layouts, attend_blocks(): lax.scan(max_step, (start_max, start_total), (kv_blocks, key_segment, key...  29.2 us
    unnamed x27, local copies, waits for them, and re-layouts  17.4 us
  transfers between devices with their start and end apart: 19, of which 11 were waited for; matrix products, arithmetic and copies ran while one was open for 12% of the time, Pallas kernels for 0%

commit v1 on v0

--- a/solution.py
+++ b/solution.py
@@ -126,7 +126,9 @@
     rows_here = tokens.shape[0]
     row_count = rows_here * lax.axis_size("seq")
     first_row = lax.axis_index("seq") * rows_here
-    gathered = lax.all_gather(tokens, "tp", axis=1, tiled=True)
+    gathered = jnp.concatenate(
+        lax.all_to_all(jnp.stack([tokens] * lax.axis_size("tp")), "tp", 0, 0), axis=1
+    )
     widened = gathered.astype(jnp.float32)
     average = jnp.mean(widened, axis=-1, keepdims=True)
     spread_sq = jnp.mean(jnp.square(widened - average), axis=-1, keepdims=True)

time: 671 us -> 643 us (0.958)
  waiting for transfers between devices: 503 us -> 453 us
  starting transfers between devices: 59.1 us -> 77.4 us
    all_gather x1 -> x0, waiting for transfers between devices: 116 us -> none  [body(): gathered = lax.all_gather(tokens, 'tp', axis=1, tiled=True)]
    all_to_all x0 -> x1, waiting for transfers between devices: none -> 50 us  [body(): lax.all_to_all(jnp.stack([tokens] * lax.axis_size('tp')), 'tp', 0, 0)]
    all_to_all x0 -> x1, starting transfers between devices: none -> 18.1 us  [body(): lax.all_to_all(jnp.stack([tokens] * lax.axis_size('tp')), 'tp', 0, 0)]
    all_gather x1, waiting for transfers between devices: 122 us -> 136 us  [body(): lax.all_gather(w_qkv, 'seq', axis=0, tiled=True)]
    unnamed x27 -> x29, local copies, waits for them, and re-layouts: 17.4 us -> 17.4 us
  transfers between devices with their start and end apart: 19 -> 19, of which waited for: 11 -> 11; matrix products, arithmetic and copies ran while one was open for 12% -> 13% of each run, Pallas kernels for 0% -> 0%
where the time goes in v1:
time: 643 us; the launch traced here: 641 us
  waiting for transfers between devices  453 us (70%)
  starting transfers between devices  77.4 us (12%)
  local copies, waits for them, and re-layouts  58.8 us (9%)
  matrix products  21.3 us (3%)
  other arithmetic  15.3 us (2%)
  between operations  13.6 us (2%)
    reduce_scatter x1, waiting for transfers between devices, body(): lax.psum_scatter(projected.astype(jnp.bfloat16), 'tp', scatter_dimension=...  144 us
    all_gather x1, waiting for transfers between devices, body(): lax.all_gather(w_qkv, 'seq', axis=0, tiled=True)  136 us
    ppermute x15, waiting for transfers between devices, from_behind(): return lax.ppermute(shard, axis, pairs)  118 us
    ppermute x15, starting transfers between devices, from_behind(): return lax.ppermute(shard, axis, pairs)  59.3 us
    all_to_all x1, waiting for transfers between devices, body(): lax.all_to_all(jnp.stack([tokens] * lax.axis_size('tp')), 'tp', 0, 0)  50 us
    squeeze x30, local copies, waits for them, and re-layouts, attend_blocks(): lax.scan(max_step, (start_max, start_total), (kv_blocks, key_segment, key...  29.3 us
    all_to_all x1, starting transfers between devices, body(): lax.all_to_all(jnp.stack([tokens] * lax.axis_size('tp')), 'tp', 0, 0)  18.1 us
    unnamed x29, local copies, waits for them, and re-layouts  17.4 us
  transfers between devices with their start and end apart: 19, of which 11 were waited for; matrix products, arithmetic and copies ran while one was open for 13% of the time, Pallas kernels for 0%

profile of v1, /device:TPU:1, one launch (start us, length us, event | category | flops | bytes accessed | tf_op | source)
XLA Modules:
  0.0 641.2 jit_solution(14735615439692431995)
XLA Ops:
  6.5 1.6 copy.66
  8.1 2.5 stack.80
  10.6 18.1 %all-to-all-start = ((bf16[8,256,512]{2,1,0:T(8,128)(2,1)}), bf16[8,256,512]{2,1,0:T(8,128)(2,1)}, u32[]{:S(2)}, u32[]{:S(2)}) async-start(bf16[8,256,512]{2,1,0:T(8,128)(2,1)} %stack.80), calls=%async_computation | async-start | bytes 4194304 | tf_op jit(solution)/shard_map/all_to_all | solution.py:130
  30.5 50.0 %all-to-all-done = bf16[8,256,512]{2,1,0:T(8,128)(2,1)} async-done(((bf16[8,256,512]{2,1,0:T(8,128)(2,1)}), bf16[8,256,512]{2,1,0:T(8,128)(2,1)}, u32[]{:S(2)}, u32[]{:S(2)}) %all-to-all-start) | async-done | bytes 2097184 | tf_op jit(solution)/shard_map/all_to_all | solution.py:130
  80.5 2.8 copy.65
  84.5 2.2 fusion.25
  86.8 136.1 %all-gather.3.cloned.1.call-done = bf16[4096,2,3,128]{3,0,2,1:T(8,128)(2,1)} async-done(((bf16[64,2,3,128]{3,0,2,1:T(8,128)(2,1)}), bf16[4096,2,3,128]{3,0,2,1:T(8,128)(2,1)}) %all-gather.3.cloned.1.call-update) | async-done | bytes 6291472 | tf_op jit(solution)/shard_map/all_gather | solution.py:141
  222.9 6.0 fusion.26
  229.0 6.4 %collective-permute-start = (bf16[256,2,2,128]{0,3,2,1:T(8,128)(2,1)S(1)}, bf16[256,2,2,128]{0,3,2,1:T(8,128)(2,1)S(1)}, u32[]{:S(2)}, u32[]{:S(2)}) collective-permute-start(bf16[256,2,2,128]{0,3,2,1:T(8,128)(2,1)S(1)} %pad_maximum_fusion.1), channel_id=1, source_target_pairs={{0,56},{8,64},{16,72},{24,80},{32,88},{40,96},{48,104},{56,112},{6... | collective-permute-start | bytes 786440 | tf_op jit(solution)/shard_map/ppermute | solution.py:14
  235.4 3.0 collective-permute-start.1
  238.5 5.3 collective-permute-start.2
  243.8 6.3 collective-permute-start.3
  250.1 1.3 collective-permute-start.4
  251.6 18.0 %collective-permute-start.5 = (bf16[256,2,2,128]{0,3,2,1:T(8,128)(2,1)S(1)}, bf16[256,2,2,128]{0,3,2,1:T(8,128)(2,1)S(1)}, u32[]{:S(2)}, u32[]{:S(2)}) collective-permute-start(bf16[256,2,2,128]{0,3,2,1:T(8,128)(2,1)S(1)} %pad_maximum_fusion.1), channel_id=1, source_target_pairs={{0,16},{8,24},{16,32},{24,40},{32,48},{40,56},{48,64},{56,72},{64,... | collective-permute-start | bytes 786440 | tf_op jit(solution)/shard_map/ppermute | solution.py:14
  270.3 5.2 collective-permute-start.6
  276.3 1.9 collective-permute-start.7
  278.9 1.3 collective-permute-start.8
  280.9 1.3 collective-permute-start.9
  282.9 1.3 collective-permute-start.10
  285.0 1.3 collective-permute-start.11
  287.7 9.0 %collective-permute-done.7 = bf16[256,2,2,128]{0,3,2,1:T(8,128)(2,1)S(1)} collective-permute-done((bf16[256,2,2,128]{0,3,2,1:T(8,128)(2,1)S(1)}, bf16[256,2,2,128]{0,3,2,1:T(8,128)(2,1)S(1)}, u32[]{:S(2)}, u32[]{:S(2)}) %collective-permute-start.7) | collective-permute-done | bytes 262176 | tf_op jit(solution)/shard_map/ppermute | solution.py:14
  296.7 1.3 collective-permute-start.12
  298.7 19.1 %collective-permute-done.8 = bf16[256,2,2,128]{0,3,2,1:T(8,128)(2,1)S(1)} collective-permute-done((bf16[256,2,2,128]{0,3,2,1:T(8,128)(2,1)S(1)}, bf16[256,2,2,128]{0,3,2,1:T(8,128)(2,1)S(1)}, u32[]{:S(2)}, u32[]{:S(2)}) %collective-permute-start.8) | collective-permute-done | bytes 262176 | tf_op jit(solution)/shard_map/ppermute | solution.py:14
  317.8 1.3 collective-permute-start.13
  319.8 21.4 %collective-permute-done.9 = bf16[256,2,2,128]{0,3,2,1:T(8,128)(2,1)S(1)} collective-permute-done((bf16[256,2,2,128]{0,3,2,1:T(8,128)(2,1)S(1)}, bf16[256,2,2,128]{0,3,2,1:T(8,128)(2,1)S(1)}, u32[]{:S(2)}, u32[]{:S(2)}) %collective-permute-start.9) | collective-permute-done | bytes 262176 | tf_op jit(solution)/shard_map/ppermute | solution.py:14
  342.7 27.1 %collective-permute-done.11 = bf16[256,2,2,128]{0,3,2,1:T(8,128)(2,1)S(1)} collective-permute-done((bf16[256,2,2,128]{0,3,2,1:T(8,128)(2,1)S(1)}, bf16[256,2,2,128]{0,3,2,1:T(8,128)(2,1)S(1)}, u32[]{:S(2)}, u32[]{:S(2)}) %collective-permute-start.11) | collective-permute-done | bytes 262176 | tf_op jit(solution)/shard_map/ppermute | solution.py:14
  370.5 11.1 %collective-permute-done.12 = bf16[256,2,2,128]{0,3,2,1:T(8,128)(2,1)S(1)} collective-permute-done((bf16[256,2,2,128]{0,3,2,1:T(8,128)(2,1)S(1)}, bf16[256,2,2,128]{0,3,2,1:T(8,128)(2,1)S(1)}, u32[]{:S(2)}, u32[]{:S(2)}) %collective-permute-start.12) | collective-permute-done | bytes 262176 | tf_op jit(solution)/shard_map/ppermute | solution.py:14
  382.3 29.0 %collective-permute-done.13 = bf16[256,2,2,128]{0,3,2,1:T(8,128)(2,1)S(1)} collective-permute-done((bf16[256,2,2,128]{0,3,2,1:T(8,128)(2,1)S(1)}, bf16[256,2,2,128]{0,3,2,1:T(8,128)(2,1)S(1)}, u32[]{:S(2)}, u32[]{:S(2)}) %collective-permute-start.13) | collective-permute-done | bytes 262176 | tf_op jit(solution)/shard_map/ppermute | solution.py:14
  412.1 6.3 copy.72
  418.3 24.1 %while.24 = (s32[]{:T(128)}, f32[2,256,1]{1,0,2:T(2,128)S(1)}, f32[2,256,1]{1,0,2:T(2,128)S(1)}, pred[256]{0:T(512)(128)(4,1)S(1)}, pred[15,256]{1,0:T(8,128)(4,...) while((s32[]{:T(128)}, f32[2,256,1]{1,0,2:T(2,128)S(1)}, ...), condition=%wide.region_9.10_spmd.clone, body=%wide.region_6.9_spmd.clone.sunk | while | flops 34540032 | bytes 2063492 | solution.py:97
  418.5 1.0 dynamic-slice_bitcast_fusion.4
  420.1 1.0 dynamic-slice_bitcast_fusion.4
  421.7 1.0 dynamic-slice_bitcast_fusion.4
  423.3 1.0 dynamic-slice_bitcast_fusion.4
  425.0 1.0 dynamic-slice_bitcast_fusion.4
  426.6 1.0 dynamic-slice_bitcast_fusion.4
  428.2 1.0 dynamic-slice_bitcast_fusion.4
  436.2 1.0 dynamic-slice_bitcast_fusion.4
  442.5 25.9 %while.25 = (s32[]{:T(128)}, f32[256,2,128]{0,2,1:T(8,128)S(1)}, bf16[15,256,2,2,128]{4,1,3,2,0:T(8,128)(2,1)}, pred[256]{0:T(512)(128)(4,1)S(1)}, pred[15,256]{...) while((s32[]{:T(128)}, f32[256,2,128]{0,2,1:T(8,128)S(1)}, ...), condition=%wide.region_11.12_spmd.clone, body=%wide.region_10.11_spmd.clone.sunk | while | flops 68222976 | bytes 1582219 | solution.py:120
  447.8 1.0 dynamic-slice_bitcast_fusion.5
  468.4 4.9 all-gather.5.cloned.1.call-done
  473.3 3.7 fusion.21
  477.4 143.7 %reduce-scatter.2.cloned.1.call-done = bf16[256,512]{1,0:T(8,128)(2,1)} async-done(((bf16[256,4096]{1,0:T(8,128)(2,1)}), bf16[256,512]{1,0:T(8,128)(2,1)}) %reduce-scatter.2.cloned.1.call-update) | async-done | bytes 262160 | tf_op jit(solution)/shard_map/reduce_scatter | solution.py:178
  621.1 1.0 add_convert_fusion
  622.1 4.1 collective-permute-start.14
  626.5 1.1 collective-permute-done.14
  627.6 4.0 gather_fusion
  631.8 2.8 select_select_fusion
  (285 shorter events, 54.6 us)
Async XLA Ops:
  6.5 23.0 %copy-start.4 = (s32[15]{0:T(128)S(1)}, s32[15]{0:T(128)}, u32[]{:S(2)}) copy-start(s32[15]{0:T(128)} %param.19) | copy-start | bytes 184
  6.5 23.3 %copy-start.5 = (s32[14]{0:T(128)S(1)}, s32[14]{0:T(128)}, u32[]{:S(2)}) copy-start(s32[14]{0:T(128)} %param.18) | copy-start | bytes 172
  6.5 216.3 %all-gather.3.cloned.1.call-start = ((), (), s32[]{:S(2)}) async-start(), calls=%async_computation.2 | async-start | bytes 6389760 | tf_op jit(solution)/shard_map/all_gather | solution.py:141
  10.6 69.9 %all-to-all-start = ((bf16[8,256,512]{2,1,0:T(8,128)(2,1)}), bf16[8,256,512]{2,1,0:T(8,128)(2,1)}, u32[]{:S(2)}, u32[]{:S(2)}) async-start(bf16[8,256,512]{2,1,0:T(8,128)(2,1)} %stack.80), calls=%async_computation | async-start | bytes 4194304 | tf_op jit(solution)/shard_map/all_to_all | solution.py:130
  28.7 444.6 %all-gather.5.cloned.1.call-start = ((), (), s32[]{:S(2)}) async-start(), calls=%async_computation.3 | async-start | bytes 2129920 | tf_op jit(solution)/shard_map/all_gather | solution.py:175
  29.4 591.6 %reduce-scatter.2.cloned.1.call-start = ((), (), s32[]{:S(2)}) async-start(), calls=%async_computation.4 | async-start | bytes 2359296 | tf_op jit(solution)/shard_map/reduce_scatter | solution.py:178
  30.5 54.1 %copy-start.1 = (f32[4096]{0:T(1024)S(1)}, f32[4096]{0:T(1024)}, u32[]{:S(2)}) copy-start(f32[4096]{0:T(1024)} %param.14) | copy-start | bytes 49156
  30.5 54.1 %copy-start.2 = (f32[4096]{0:T(1024)S(1)}, f32[4096]{0:T(1024)}, u32[]{:S(2)}) copy-start(f32[4096]{0:T(1024)} %param.13) | copy-start | bytes 49156
  229.0 22.6 %collective-permute-start = (bf16[256,2,2,128]{0,3,2,1:T(8,128)(2,1)S(1)}, bf16[256,2,2,128]{0,3,2,1:T(8,128)(2,1)S(1)}, u32[]{:S(2)}, u32[]{:S(2)}) collective-permute-start(bf16[256,2,2,128]{0,3,2,1:T(8,128)(2,1)S(1)} %pad_maximum_fusion.1), channel_id=1, source_target_pairs={{0,56},{8,64},{16,72},{24,80},{32,88},{40,96},{48,104},{56,112},{6... | collective-permute-start | bytes 786440 | tf_op jit(solution)/shard_map/ppermute | solution.py:14
  235.4 34.9 %collective-permute-start.1 = (bf16[256,2,2,128]{0,3,2,1:T(8,128)(2,1)S(1)}, bf16[256,2,2,128]{0,3,2,1:T(8,128)(2,1)S(1)}, u32[]{:S(2)}, u32[]{:S(2)}) collective-permute-start(bf16[256,2,2,128]{0,3,2,1:T(8,128)(2,1)S(1)} %pad_maximum_fusion.1), channel_id=1, source_target_pairs={{0,48},{8,56},{16,64},{24,72},{32,80},{40,88},{48,96},{56,104},{64... | collective-permute-start | bytes 786440 | tf_op jit(solution)/shard_map/ppermute | solution.py:14
  238.5 37.8 %collective-permute-start.2 = (bf16[256,2,2,128]{0,3,2,1:T(8,128)(2,1)S(1)}, bf16[256,2,2,128]{0,3,2,1:T(8,128)(2,1)S(1)}, u32[]{:S(2)}, u32[]{:S(2)}) collective-permute-start(bf16[256,2,2,128]{0,3,2,1:T(8,128)(2,1)S(1)} %pad_maximum_fusion.1), channel_id=1, source_target_pairs={{0,40},{8,48},{16,56},{24,64},{32,72},{40,80},{48,88},{56,96},{64,... | collective-permute-start | bytes 786440 | tf_op jit(solution)/shard_map/ppermute | solution.py:14
  243.8 35.1 %collective-permute-start.3 = (bf16[256,2,2,128]{0,3,2,1:T(8,128)(2,1)S(1)}, bf16[256,2,2,128]{0,3,2,1:T(8,128)(2,1)S(1)}, u32[]{:S(2)}, u32[]{:S(2)}) collective-permute-start(bf16[256,2,2,128]{0,3,2,1:T(8,128)(2,1)S(1)} %pad_maximum_fusion.1), channel_id=1, source_target_pairs={{0,32},{8,40},{16,48},{24,56},{32,64},{40,72},{48,80},{56,88},{64,... | collective-permute-start | bytes 786440 | tf_op jit(solution)/shard_map/ppermute | solution.py:14
  250.1 30.8 %collective-permute-start.4 = (bf16[256,2,2,128]{0,3,2,1:T(8,128)(2,1)S(1)}, bf16[256,2,2,128]{0,3,2,1:T(8,128)(2,1)S(1)}, u32[]{:S(2)}, u32[]{:S(2)}) collective-permute-start(bf16[256,2,2,128]{0,3,2,1:T(8,128)(2,1)S(1)} %pad_maximum_fusion.1), channel_id=1, source_target_pairs={{0,24},{8,32},{16,40},{24,48},{32,56},{40,64},{48,72},{56,80},{64,... | collective-permute-start | bytes 786440 | tf_op jit(solution)/shard_map/ppermute | solution.py:14
  251.6 31.3 %collective-permute-start.5 = (bf16[256,2,2,128]{0,3,2,1:T(8,128)(2,1)S(1)}, bf16[256,2,2,128]{0,3,2,1:T(8,128)(2,1)S(1)}, u32[]{:S(2)}, u32[]{:S(2)}) collective-permute-start(bf16[256,2,2,128]{0,3,2,1:T(8,128)(2,1)S(1)} %pad_maximum_fusion.1), channel_id=1, source_target_pairs={{0,16},{8,24},{16,32},{24,40},{32,48},{40,56},{48,64},{56,72},{64,... | collective-permute-start | bytes 786440 | tf_op jit(solution)/shard_map/ppermute | solution.py:14
  270.3 14.6 %collective-permute-start.6 = (bf16[256,2,2,128]{0,3,2,1:T(8,128)(2,1)S(1)}, bf16[256,2,2,128]{0,3,2,1:T(8,128)(2,1)S(1)}, u32[]{:S(2)}, u32[]{:S(2)}) collective-permute-start(bf16[256,2,2,128]{0,3,2,1:T(8,128)(2,1)S(1)} %pad_maximum_fusion.1), channel_id=1, source_target_pairs={{0,8},{8,16},{16,24},{24,32},{32,40},{40,48},{48,56},{56,64},{64,7... | collective-permute-start | bytes 786440 | tf_op jit(solution)/shard_map/ppermute | solution.py:14
  276.3 20.4 %collective-permute-start.7 = (bf16[256,2,2,128]{0,3,2,1:T(8,128)(2,1)S(1)}, bf16[256,2,2,128]{0,3,2,1:T(8,128)(2,1)S(1)}, u32[]{:S(2)}, u32[]{:S(2)}) collective-permute-start(bf16[256,2,2,128]{0,3,2,1:T(8,128)(2,1)S(1)} %pad_maximum_fusion.1), channel_id=1, source_target_pairs={{8,0},{16,8},{24,16},{32,24},{40,32},{48,40},{56,48},{64,56},{72,6... | collective-permute-start | bytes 786440 | tf_op jit(solution)/shard_map/ppermute | solution.py:14
  278.9 38.9 %collective-permute-start.8 = (bf16[256,2,2,128]{0,3,2,1:T(8,128)(2,1)S(1)}, bf16[256,2,2,128]{0,3,2,1:T(8,128)(2,1)S(1)}, u32[]{:S(2)}, u32[]{:S(2)}) collective-permute-start(bf16[256,2,2,128]{0,3,2,1:T(8,128)(2,1)S(1)} %pad_maximum_fusion.1), channel_id=1, source_target_pairs={{16,0},{24,8},{32,16},{40,24},{48,32},{56,40},{64,48},{72,56},{80,... | collective-permute-start | bytes 786440 | tf_op jit(solution)/shard_map/ppermute | solution.py:14
  280.9 60.3 %collective-permute-start.9 = (bf16[256,2,2,128]{0,3,2,1:T(8,128)(2,1)S(1)}, bf16[256,2,2,128]{0,3,2,1:T(8,128)(2,1)S(1)}, u32[]{:S(2)}, u32[]{:S(2)}) collective-permute-start(bf16[256,2,2,128]{0,3,2,1:T(8,128)(2,1)S(1)} %pad_maximum_fusion.1), channel_id=1, source_target_pairs={{24,0},{32,8},{40,16},{48,24},{56,32},{64,40},{72,48},{80,56},{88,... | collective-permute-start | bytes 786440 | tf_op jit(solution)/shard_map/ppermute | solution.py:14
  282.9 59.0 %collective-permute-start.10 = (bf16[256,2,2,128]{0,3,2,1:T(8,128)(2,1)S(1)}, bf16[256,2,2,128]{0,3,2,1:T(8,128)(2,1)S(1)}, u32[]{:S(2)}, u32[]{:S(2)}) collective-permute-start(bf16[256,2,2,128]{0,3,2,1:T(8,128)(2,1)S(1)} %pad_maximum_fusion.1), channel_id=1, source_target_pairs={{32,0},{40,8},{48,16},{56,24},{64,32},{72,40},{80,48},{88,56},{96,... | collective-permute-start | bytes 786440 | tf_op jit(solution)/shard_map/ppermute | solution.py:14
  285.0 84.8 %collective-permute-start.11 = (bf16[256,2,2,128]{0,3,2,1:T(8,128)(2,1)S(1)}, bf16[256,2,2,128]{0,3,2,1:T(8,128)(2,1)S(1)}, u32[]{:S(2)}, u32[]{:S(2)}) collective-permute-start(bf16[256,2,2,128]{0,3,2,1:T(8,128)(2,1)S(1)} %pad_maximum_fusion.1), channel_id=1, source_target_pairs={{40,0},{48,8},{56,16},{64,24},{72,32},{80,40},{88,48},{96,56},{104... | collective-permute-start | bytes 786440 | tf_op jit(solution)/shard_map/ppermute | solution.py:14
  296.7 84.9 %collective-permute-start.12 = (bf16[256,2,2,128]{0,3,2,1:T(8,128)(2,1)S(1)}, bf16[256,2,2,128]{0,3,2,1:T(8,128)(2,1)S(1)}, u32[]{:S(2)}, u32[]{:S(2)}) collective-permute-start(bf16[256,2,2,128]{0,3,2,1:T(8,128)(2,1)S(1)} %pad_maximum_fusion.1), channel_id=1, source_target_pairs={{48,0},{56,8},{64,16},{72,24},{80,32},{88,40},{96,48},{104,56},{11... | collective-permute-start | bytes 786440 | tf_op jit(solution)/shard_map/ppermute | solution.py:14
  317.8 93.5 %collective-permute-start.13 = (bf16[256,2,2,128]{0,3,2,1:T(8,128)(2,1)S(1)}, bf16[256,2,2,128]{0,3,2,1:T(8,128)(2,1)S(1)}, u32[]{:S(2)}, u32[]{:S(2)}) collective-permute-start(bf16[256,2,2,128]{0,3,2,1:T(8,128)(2,1)S(1)} %pad_maximum_fusion.1), channel_id=1, source_target_pairs={{56,0},{64,8},{72,16},{80,24},{88,32},{96,40},{104,48},{112,56},{1... | collective-permute-start | bytes 786440 | tf_op jit(solution)/shard_map/ppermute | solution.py:14
  468.4 152.7 %copy-start = (bf16[256,512]{1,0:T(8,128)(2,1)S(1)}, bf16[256,512]{1,0:T(8,128)(2,1)}, u32[]{:S(2)}) copy-start(bf16[256,512]{1,0:T(8,128)(2,1)} %param.12) | copy-start | bytes 786436
  468.4 152.7 %copy-start.3 = (f32[512]{0:T(512)S(1)}, f32[512]{0:T(512)}, u32[]{:S(2)}) copy-start(f32[512]{0:T(512)} %param.17) | copy-start | bytes 6148
  622.1 5.4 collective-permute-start.14
Sparse Core Ops, SparseCore 0:
  9.5 213.3 all-gather.2
  225.0 248.2 all-gather.4
  478.0 143.0 reduce-scatter.1
